TPU v7x, 32 devices: a whole 2x2x4 slice. The times are simulated.
32 devices in a mesh: tx: 16 (over z, y, x), ty: 2 (over core).
Axes of the slice: x: 2, y: 2, z: 4, core: 2. Of those that a mesh axis runs over, the one named last changes fastest.
Arguments:
- pulses: bfloat16 [32, 2, 16384], P(('tx', 'ty')), may hold values from -6 to 6
- geometry: bfloat16 [5, 32], P(None, ('tx', 'ty')), as said below
- footprint: int32 [32, 8], P(('tx', 'ty')), may hold values from 0 to 15, as said below
- offsets: int32 [32, 16], P(None, 'tx'), may hold values from 0 to 15352
- image_in: float32 [2, 8192, 1024], P(None, 'tx', 'ty'), may hold values from -6 to 6
Outputs:
- image_out: float32 [2, 8192, 1024], P(None, 'tx', 'ty')
Inputs may be any that keep to these rules, and one draw needn't show every extreme that they name: `footprint`: each row is a run of 8 consecutive tile-row indices in ascending order. `geometry`: row 0 lies in 0.002 to 0.05, rows 1 and 4 in -pi to pi, row 2 in -0.05 to 0.05, row 3 in -0.02 to 0.02.
All inputs are finite; a program needn't handle non-finite values.
Results may differ from a plain program's by a relative error of at most 0.0027.
Values may be sent and summed in bfloat16 or wider, within the bound.
No kernel may reach another device: no remote copies, remote signals or barrier semaphores. Data moves between devices by JAX's collectives and lax.ppermute only.
A program may use at most 64 MiB of HBM per device.

v0:
```python
import math
import jax
import jax.numpy as jnp
from jax import lax
from jax.sharding import PartitionSpec as P

TAPS = 8


def make_taps(geometry, columns):
    rate = geometry[0].astype(jnp.float32)[:, None]
    shift = geometry[1].astype(jnp.float32)[:, None]
    ramp = geometry[2].astype(jnp.float32)[:, None]
    fraction = 0.5 + 0.45 * jnp.sin(rate * columns[None, :] + shift)
    places = jnp.arange(TAPS).astype(jnp.float32)
    spread = places[None, :, None] - 3.0 - fraction[:, None, :]
    angle_x = jnp.pi * spread
    kernel = jnp.sin(angle_x) / angle_x * (0.54 + 0.46 * jnp.cos(angle_x / 4.0))
    turning = ramp * columns[None, :]
    real_part = kernel * jnp.cos(turning)[:, None, :]
    imag_part = kernel * jnp.sin(turning)[:, None, :]
    return jnp.concatenate([real_part, imag_part], axis=1).astype(jnp.bfloat16)


def interpolate(windows, taps, width):
    real_sum = jnp.zeros((windows.shape[0], width), jnp.float32)
    imag_sum = jnp.zeros((windows.shape[0], width), jnp.float32)
    for k in range(TAPS):
        segment = windows[:, :, k : k + width].astype(jnp.float32)
        tap_real = taps[:, k].astype(jnp.float32)
        tap_imag = taps[:, TAPS + k].astype(jnp.float32)
        real_sum = real_sum + tap_real * segment[:, 0] - tap_imag * segment[:, 1]
        imag_sum = imag_sum + tap_real * segment[:, 1] + tap_imag * segment[:, 0]
    return jnp.concatenate([real_sum, imag_sum], axis=0).astype(jnp.bfloat16)


def phase_matrix(tilt, base_phase, rows):
    angles = (
        rows[:, None] * tilt.astype(jnp.float32)[None, :] + base_phase.astype(jnp.float32)[None, :]
    )
    cosine = jnp.cos(angles).astype(jnp.bfloat16)
    sine = jnp.sin(angles).astype(jnp.bfloat16)
    upper = jnp.concatenate([cosine, -sine], axis=1)
    lower = jnp.concatenate([sine, cosine], axis=1)
    return jnp.concatenate([upper, lower], axis=0)


def body(pulses, geometry, footprint, offsets, image_in):
    count_rows = lax.axis_size("tx")
    count_cols = lax.axis_size("ty")
    devices_all = count_rows * count_cols
    held = pulses.shape[0]
    tile_rows_n = image_in.shape[1]
    tile_cols_n = image_in.shape[2]
    length = tile_cols_n + TAPS
    wide_length = count_cols * tile_cols_n + TAPS
    myself = lax.axis_index("tx") * count_cols + lax.axis_index("ty")
    all_offsets = lax.all_gather(offsets, "tx", axis=1, tiled=True)
    mine = lax.dynamic_slice_in_dim(all_offsets, myself * held, held, 0)
    live = jnp.any(
        footprint[:, :, None] == jnp.arange(count_rows, dtype=jnp.int32)[None, None, :], axis=1
    )
    live_rows = live.T[:, None, :, None, None]

    def cut_window(signal, start):
        return lax.dynamic_slice_in_dim(signal, start, wide_length, 1)

    per_pulse = jax.vmap(cut_window, in_axes=(0, 0))
    per_row = jax.vmap(per_pulse, in_axes=(None, 0))
    row_windows = per_row(pulses, mine.T)
    pieces = [
        row_windows[:, :, :, j * tile_cols_n : j * tile_cols_n + length] for j in range(count_cols)
    ]
    windows = jnp.stack(pieces, axis=1)
    windows = jnp.where(live_rows, windows, jnp.zeros((), windows.dtype))
    windows = windows.reshape(devices_all, held, 2, length)
    slots = devices_all * held
    geo_send = jnp.broadcast_to(geometry.T[None], (devices_all, held, 5))
    got_windows, got_geo = (
        lax.all_to_all(windows, ("tx", "ty"), split_axis=0, concat_axis=0, tiled=True),
        lax.all_to_all(geo_send, ("tx", "ty"), split_axis=0, concat_axis=0, tiled=True),
    )
    got_geo = got_geo.reshape(slots, 5).T
    columns = (
        lax.axis_index("ty") * tile_cols_n + jnp.arange(tile_cols_n, dtype=jnp.int32)
    ).astype(jnp.float32)
    got_taps = make_taps(got_geo, columns)
    row_geo = got_geo[3:5]
    got_windows = got_windows.reshape(slots, 2, length)
    values = interpolate(got_windows, got_taps, tile_cols_n)
    rows = (lax.axis_index("tx") * tile_rows_n + jnp.arange(tile_rows_n, dtype=jnp.int32)).astype(
        jnp.float32
    )
    left = phase_matrix(row_geo[0], row_geo[1], rows)
    product = jnp.dot(left, values, preferred_element_type=jnp.float32).reshape(
        2, tile_rows_n, tile_cols_n
    )
    scale = 1.0 / math.sqrt(slots)
    return image_in + scale * product


def solution(mesh):
    in_specs = (
        P(("tx", "ty"), None, None),
        P(None, ("tx", "ty")),
        P(("tx", "ty"), None),
        P(None, "tx"),
        P(None, "tx", "ty"),
    )
    out_specs = P(None, "tx", "ty")
    return jax.shard_map(body, mesh=mesh, in_specs=in_specs, out_specs=out_specs, check_vma=False)
```

profile of v0, /device:TPU:0, one launch (start us, length us, event | category | flops | bytes accessed | tf_op | source)
XLA Modules:
  0.0 98.0 jit_solution(8685950877705287480)
XLA Ops:
  0.0 1.3 %broadcast_in_dim.21 = bf16[32,1,5]{2,1,0:T(2,128)(2,1)} broadcast(bf16[5]{0:T(256)(128)(2,1)} %bitcast.67), dimensions={2} | broadcast | bytes 330 | tf_op jit(solution)/shard_map/broadcast_in_dim | solution.py:78
  1.3 7.3 %all-to-all-start = ((bf16[32,1,5]{2,1,0:T(2,128)(2,1)}), bf16[32,1,5]{2,1,0:T(2,128)(2,1)S(1)}, u32[]{:S(2)}, u32[]{:S(2)}) async-start(bf16[32,1,5]{2,1,0:T(2,128)(2,1)} %broadcast_in_dim.21), calls=%async_computation | async-start | bytes 32768 | tf_op jit(solution)/shard_map/all_to_all | solution.py:81
  8.6 0.7 fusion.51
  9.5 40.9 %all-gather = s32[16,1,32]{2,1,0:T(1,128)S(1)} all-gather(s32[1,1,32]{2,1,0:T(1,128)} %bitcast.68), channel_id=1, replica_groups=mesh['tx'=16,'ty'=2] {'tx'}, dimensions={0}, use_global_device_ids=true | all-gather | bytes 2176 | tf_op jit(solution)/shard_map/all_gather | solution.py:58
  50.6 32.4 %while.1 = (s32[]{:T(128)}, bf16[1,2,16384]{2,1,0:T(2,128)(2,1)}, s32[16,3]{0,1:T(4,128)S(1)}, bf16[16,2,1032]{2,1,0:T(2,128)(2,1)S(1)}, s32[]{:T(128)}) while((s32[]{:T(128)}, bf16[1,2,16384]{2,1,0:T(2,128)(2,1)}, s32[16,3]{0,1:T(4,128)S(1)}, bf16[16,2,1032]{2,1,0:T(2,128)(2,1)S(1)}, s32[]{:T(128)}) %tuple.32), condition=%wide.while_cond, body=%wide.while_body.sunk | while | flops 2 | bytes 8849 | solution.py:66
  50.7 0.5 slice.359
  51.2 1.4 %dynamic-slice_dynamic-update-slice_fusion.2 = bf16[16,2,1032]{2,1,0:T(2,128)(2,1)S(1)} fusion(bf16[16,2,1032]{2,1,0:T(2,128)(2,1)S(1)} %get-tuple-element.76, s32[]{:T(128)S(6)} %copy.86, bf16[1,2,16384]{2,1,0:T(2,128)(2,1)} %get-tuple-element.79, s32[]{:T(128)} %bitcast.61), kind=kLoop, calls=%fused_computation.clone.1 | loop fusion | bytes 8744 | tf_op jit(solution)/shard_map/vmap(vmap())/gather
  52.7 0.5 slice.359
  53.2 1.4 %dynamic-slice_dynamic-update-slice_fusion.2 = bf16[16,2,1032]{2,1,0:T(2,128)(2,1)S(1)} fusion(bf16[16,2,1032]{2,1,0:T(2,128)(2,1)S(1)} %get-tuple-element.76, s32[]{:T(128)S(6)} %copy.86, bf16[1,2,16384]{2,1,0:T(2,128)(2,1)} %get-tuple-element.79, s32[]{:T(128)} %bitcast.61), kind=kLoop, calls=%fused_computation.clone.1 | loop fusion | bytes 8744 | tf_op jit(solution)/shard_map/vmap(vmap())/gather
  54.7 0.5 slice.359
  55.3 1.4 %dynamic-slice_dynamic-update-slice_fusion.2 = bf16[16,2,1032]{2,1,0:T(2,128)(2,1)S(1)} fusion(bf16[16,2,1032]{2,1,0:T(2,128)(2,1)S(1)} %get-tuple-element.76, s32[]{:T(128)S(6)} %copy.86, bf16[1,2,16384]{2,1,0:T(2,128)(2,1)} %get-tuple-element.79, s32[]{:T(128)} %bitcast.61), kind=kLoop, calls=%fused_computation.clone.1 | loop fusion | bytes 8744 | tf_op jit(solution)/shard_map/vmap(vmap())/gather
  56.7 0.5 slice.359
  57.3 1.4 %dynamic-slice_dynamic-update-slice_fusion.2 = bf16[16,2,1032]{2,1,0:T(2,128)(2,1)S(1)} fusion(bf16[16,2,1032]{2,1,0:T(2,128)(2,1)S(1)} %get-tuple-element.76, s32[]{:T(128)S(6)} %copy.86, bf16[1,2,16384]{2,1,0:T(2,128)(2,1)} %get-tuple-element.79, s32[]{:T(128)} %bitcast.61), kind=kLoop, calls=%fused_computation.clone.1 | loop fusion | bytes 8744 | tf_op jit(solution)/shard_map/vmap(vmap())/gather
  58.8 0.5 slice.359
  59.3 1.4 %dynamic-slice_dynamic-update-slice_fusion.2 = bf16[16,2,1032]{2,1,0:T(2,128)(2,1)S(1)} fusion(bf16[16,2,1032]{2,1,0:T(2,128)(2,1)S(1)} %get-tuple-element.76, s32[]{:T(128)S(6)} %copy.86, bf16[1,2,16384]{2,1,0:T(2,128)(2,1)} %get-tuple-element.79, s32[]{:T(128)} %bitcast.61), kind=kLoop, calls=%fused_computation.clone.1 | loop fusion | bytes 8744 | tf_op jit(solution)/shard_map/vmap(vmap())/gather
  60.8 0.5 slice.359
  61.3 1.4 %dynamic-slice_dynamic-update-slice_fusion.2 = bf16[16,2,1032]{2,1,0:T(2,128)(2,1)S(1)} fusion(bf16[16,2,1032]{2,1,0:T(2,128)(2,1)S(1)} %get-tuple-element.76, s32[]{:T(128)S(6)} %copy.86, bf16[1,2,16384]{2,1,0:T(2,128)(2,1)} %get-tuple-element.79, s32[]{:T(128)} %bitcast.61), kind=kLoop, calls=%fused_computation.clone.1 | loop fusion | bytes 8744 | tf_op jit(solution)/shard_map/vmap(vmap())/gather
  62.8 0.5 slice.359
  63.4 1.4 %dynamic-slice_dynamic-update-slice_fusion.2 = bf16[16,2,1032]{2,1,0:T(2,128)(2,1)S(1)} fusion(bf16[16,2,1032]{2,1,0:T(2,128)(2,1)S(1)} %get-tuple-element.76, s32[]{:T(128)S(6)} %copy.86, bf16[1,2,16384]{2,1,0:T(2,128)(2,1)} %get-tuple-element.79, s32[]{:T(128)} %bitcast.61), kind=kLoop, calls=%fused_computation.clone.1 | loop fusion | bytes 8744 | tf_op jit(solution)/shard_map/vmap(vmap())/gather
  64.8 0.5 slice.359
  65.4 1.4 %dynamic-slice_dynamic-update-slice_fusion.2 = bf16[16,2,1032]{2,1,0:T(2,128)(2,1)S(1)} fusion(bf16[16,2,1032]{2,1,0:T(2,128)(2,1)S(1)} %get-tuple-element.76, s32[]{:T(128)S(6)} %copy.86, bf16[1,2,16384]{2,1,0:T(2,128)(2,1)} %get-tuple-element.79, s32[]{:T(128)} %bitcast.61), kind=kLoop, calls=%fused_computation.clone.1 | loop fusion | bytes 8744 | tf_op jit(solution)/shard_map/vmap(vmap())/gather
  66.9 0.5 slice.359
  67.4 1.4 %dynamic-slice_dynamic-update-slice_fusion.2 = bf16[16,2,1032]{2,1,0:T(2,128)(2,1)S(1)} fusion(bf16[16,2,1032]{2,1,0:T(2,128)(2,1)S(1)} %get-tuple-element.76, s32[]{:T(128)S(6)} %copy.86, bf16[1,2,16384]{2,1,0:T(2,128)(2,1)} %get-tuple-element.79, s32[]{:T(128)} %bitcast.61), kind=kLoop, calls=%fused_computation.clone.1 | loop fusion | bytes 8744 | tf_op jit(solution)/shard_map/vmap(vmap())/gather
  68.9 0.5 slice.359
  69.4 1.4 %dynamic-slice_dynamic-update-slice_fusion.2 = bf16[16,2,1032]{2,1,0:T(2,128)(2,1)S(1)} fusion(bf16[16,2,1032]{2,1,0:T(2,128)(2,1)S(1)} %get-tuple-element.76, s32[]{:T(128)S(6)} %copy.86, bf16[1,2,16384]{2,1,0:T(2,128)(2,1)} %get-tuple-element.79, s32[]{:T(128)} %bitcast.61), kind=kLoop, calls=%fused_computation.clone.1 | loop fusion | bytes 8744 | tf_op jit(solution)/shard_map/vmap(vmap())/gather
  70.9 0.5 slice.359
  71.5 1.4 %dynamic-slice_dynamic-update-slice_fusion.2 = bf16[16,2,1032]{2,1,0:T(2,128)(2,1)S(1)} fusion(bf16[16,2,1032]{2,1,0:T(2,128)(2,1)S(1)} %get-tuple-element.76, s32[]{:T(128)S(6)} %copy.86, bf16[1,2,16384]{2,1,0:T(2,128)(2,1)} %get-tuple-element.79, s32[]{:T(128)} %bitcast.61), kind=kLoop, calls=%fused_computation.clone.1 | loop fusion | bytes 8744 | tf_op jit(solution)/shard_map/vmap(vmap())/gather
  72.9 0.5 slice.359
  73.5 1.4 %dynamic-slice_dynamic-update-slice_fusion.2 = bf16[16,2,1032]{2,1,0:T(2,128)(2,1)S(1)} fusion(bf16[16,2,1032]{2,1,0:T(2,128)(2,1)S(1)} %get-tuple-element.76, s32[]{:T(128)S(6)} %copy.86, bf16[1,2,16384]{2,1,0:T(2,128)(2,1)} %get-tuple-element.79, s32[]{:T(128)} %bitcast.61), kind=kLoop, calls=%fused_computation.clone.1 | loop fusion | bytes 8744 | tf_op jit(solution)/shard_map/vmap(vmap())/gather
  75.0 0.5 slice.359
  75.5 1.4 %dynamic-slice_dynamic-update-slice_fusion.2 = bf16[16,2,1032]{2,1,0:T(2,128)(2,1)S(1)} fusion(bf16[16,2,1032]{2,1,0:T(2,128)(2,1)S(1)} %get-tuple-element.76, s32[]{:T(128)S(6)} %copy.86, bf16[1,2,16384]{2,1,0:T(2,128)(2,1)} %get-tuple-element.79, s32[]{:T(128)} %bitcast.61), kind=kLoop, calls=%fused_computation.clone.1 | loop fusion | bytes 8744 | tf_op jit(solution)/shard_map/vmap(vmap())/gather
  77.0 0.5 slice.359
  77.5 1.4 %dynamic-slice_dynamic-update-slice_fusion.2 = bf16[16,2,1032]{2,1,0:T(2,128)(2,1)S(1)} fusion(bf16[16,2,1032]{2,1,0:T(2,128)(2,1)S(1)} %get-tuple-element.76, s32[]{:T(128)S(6)} %copy.86, bf16[1,2,16384]{2,1,0:T(2,128)(2,1)} %get-tuple-element.79, s32[]{:T(128)} %bitcast.61), kind=kLoop, calls=%fused_computation.clone.1 | loop fusion | bytes 8744 | tf_op jit(solution)/shard_map/vmap(vmap())/gather
  79.0 0.5 slice.359
  79.6 1.4 %dynamic-slice_dynamic-update-slice_fusion.2 = bf16[16,2,1032]{2,1,0:T(2,128)(2,1)S(1)} fusion(bf16[16,2,1032]{2,1,0:T(2,128)(2,1)S(1)} %get-tuple-element.76, s32[]{:T(128)S(6)} %copy.86, bf16[1,2,16384]{2,1,0:T(2,128)(2,1)} %get-tuple-element.79, s32[]{:T(128)} %bitcast.61), kind=kLoop, calls=%fused_computation.clone.1 | loop fusion | bytes 8744 | tf_op jit(solution)/shard_map/vmap(vmap())/gather
  81.0 0.5 slice.359
  81.6 1.4 %dynamic-slice_dynamic-update-slice_fusion.2 = bf16[16,2,1032]{2,1,0:T(2,128)(2,1)S(1)} fusion(bf16[16,2,1032]{2,1,0:T(2,128)(2,1)S(1)} %get-tuple-element.76, s32[]{:T(128)S(6)} %copy.86, bf16[1,2,16384]{2,1,0:T(2,128)(2,1)} %get-tuple-element.79, s32[]{:T(128)} %bitcast.61), kind=kLoop, calls=%fused_computation.clone.1 | loop fusion | bytes 8744 | tf_op jit(solution)/shard_map/vmap(vmap())/gather
  83.3 0.8 fusion.11
  84.1 2.6 %all-to-all-start.1 = ((bf16[32,1,2,520]{3,2,1,0:T(2,128)(2,1)}), bf16[32,1,2,520]{3,2,1,0:T(2,128)(2,1)S(1)}, u32[]{:S(2)}, u32[]{:S(2)}) async-start(bf16[32,1,2,520]{3,2,1,0:T(2,128)(2,1)} %fusion.11), calls=%async_computation.1 | async-start | bytes 163840 | tf_op jit(solution)/shard_map/all_to_all | solution.py:80
  86.7 0.3 sine_convert_fusion
  87.1 0.5 multiply_cosine_fusion
  87.6 3.8 %multiply_convert_fusion.1 = (bf16[32,8,512]{2,0,1:T(8,128)(2,1)S(1)}, bf16[32,8,512]{2,0,1:T(8,128)(2,1)S(1)}) fusion(f32[32,512]{1,0:T(8,128)S(1)} %get-tuple-element.35, f32[32,512]{1,0:T(8,128)S(1)} %get-tuple-element.37, f32[8]{0:T(128)S(1)} %convert_add_fusion, f32[32,512]{1,0:T(8,128)S(1)} %get-tuple-element.36), kind=kLoop, calls=%fused_computation.11 | loop fusion | flops 1441792 | bytes 720928 | tf_op jit(solution)/shard_map/convert.7
  91.4 0.3 fusion.53
  91.7 2.6 %all-to-all-done.1 = bf16[32,1,2,520]{3,2,1,0:T(2,128)(2,1)S(1)} async-done(((bf16[32,1,2,520]{3,2,1,0:T(2,128)(2,1)}), bf16[32,1,2,520]{3,2,1,0:T(2,128)(2,1)S(1)}, u32[]{:S(2)}, u32[]{:S(2)}) %all-to-all-start.1) | async-done | bytes 66592 | tf_op jit(solution)/shard_map/all_to_all | solution.py:80
  94.3 0.2 slice_convert_fusion.7
  94.8 0.5 convolution_multiply_fusion
  95.3 0.9 copy-done
  96.2 1.8 %add.204 = f32[2,512,512]{2,1,0:T(8,128)} add(f32[2,512,512]{2,1,0:T(8,128)S(1)} %copy-done, f32[2,512,512]{2,1,0:T(8,128)S(1)} %bitcast.62) | non-fusion elementwise | flops 524288 | bytes 6291456 | tf_op jit(solution)/shard_map/add | solution.py:99
  (35 shorter events, 2.2 us)
Async XLA Ops:
  1.3 82.8 %all-to-all-start = ((bf16[32,1,5]{2,1,0:T(2,128)(2,1)}), bf16[32,1,5]{2,1,0:T(2,128)(2,1)S(1)}, u32[]{:S(2)}, u32[]{:S(2)}) async-start(bf16[32,1,5]{2,1,0:T(2,128)(2,1)} %broadcast_in_dim.21), calls=%async_computation | async-start | bytes 32768 | tf_op jit(solution)/shard_map/all_to_all | solution.py:81
  84.1 10.2 %all-to-all-start.1 = ((bf16[32,1,2,520]{3,2,1,0:T(2,128)(2,1)}), bf16[32,1,2,520]{3,2,1,0:T(2,128)(2,1)S(1)}, u32[]{:S(2)}, u32[]{:S(2)}) async-start(bf16[32,1,2,520]{3,2,1,0:T(2,128)(2,1)} %fusion.11), calls=%async_computation.1 | async-start | bytes 163840 | tf_op jit(solution)/shard_map/all_to_all | solution.py:80
  94.6 1.6 %copy-start = (f32[2,512,512]{2,1,0:T(8,128)S(1)}, f32[2,512,512]{2,1,0:T(8,128)}, u32[]{:S(2)}) copy-start(f32[2,512,512]{2,1,0:T(8,128)} %param.9) | copy-start | bytes 6291460
where the time goes:
time: 99 us; the launch traced here: 98 us
  blocking collectives  40.9 us (41%)
  local copies, waits for them, and re-layouts  35.1 us (35%)
  starting transfers between devices  9.87 us (10%)
  other arithmetic  9.01 us (9%)
  waiting for transfers between devices  2.57 us (3%)
    all_gather x1, blocking collectives, body(): all_offsets = lax.all_gather(offsets, 'tx', axis=1, tiled=True)  40.9 us
    gather x48, local copies, waits for them, and re-layouts  32.4 us
    all_to_all x1, starting transfers between devices, body(): lax.all_to_all(geo_send, ('tx', 'ty'), split_axis=0, concat_axis=0, tiled...  7.3 us
    another operation x3, other arithmetic  4.1 us
    all_to_all x1, starting transfers between devices, body(): lax.all_to_all(windows, ('tx', 'ty'), split_axis=0, concat_axis=0, tiled=...  2.57 us
    all_to_all x1, waiting for transfers between devices, body(): lax.all_to_all(windows, ('tx', 'ty'), split_axis=0, concat_axis=0, tiled=...  2.56 us
  transfers between devices with their start and end apart: 2, of which 1 were waited for; matrix products, arithmetic and copies ran while one was open for 40% of the time, Pallas kernels for 0%

commit v1 on v0

--- a/solution.py
+++ b/solution.py
@@ -5,6 +5,19 @@
 from jax.sharding import PartitionSpec as P
 
 TAPS = 8
+
+
+def gather_around(x, axis, dim):
+    ways = lax.axis_size(axis)
+    up = [(d, (d + 1) % ways) for d in range(ways)]
+    down = [(d, (d - 1) % ways) for d in range(ways)]
+    earlier, later = ([x], [x])
+    for _ in range(ways // 2):
+        earlier.append(lax.ppermute(earlier[-1], axis, up))
+    for _ in range((ways - 1) // 2):
+        later.append(lax.ppermute(later[-1], axis, down))
+    line = jnp.concatenate([*earlier[::-1], *later[1:]], axis=dim)
+    return jnp.roll(line, (lax.axis_index(axis) - ways // 2) * x.shape[dim], axis=dim)
 
 
 def make_taps(geometry, columns):
@@ -55,7 +68,7 @@
     length = tile_cols_n + TAPS
     wide_length = count_cols * tile_cols_n + TAPS
     myself = lax.axis_index("tx") * count_cols + lax.axis_index("ty")
-    all_offsets = lax.all_gather(offsets, "tx", axis=1, tiled=True)
+    all_offsets = gather_around(offsets, "tx", 1)
     mine = lax.dynamic_slice_in_dim(all_offsets, myself * held, held, 0)
     live = jnp.any(
         footprint[:, :, None] == jnp.arange(count_rows, dtype=jnp.int32)[None, None, :], axis=1

time: 99 us -> 115 us (1.16)
  blocking collectives: 40.9 us -> 0 us
  starting transfers between devices: 9.87 us -> 45.9 us
  waiting for transfers between devices: 2.57 us -> 21.7 us
  local copies, waits for them, and re-layouts: 35.1 us -> 36.4 us
    all_gather x1 -> x0, blocking collectives: 40.9 us -> none  [body(): all_offsets = lax.all_gather(offsets, 'tx', axis=1, tiled=True)]
    ppermute x0 -> x15, starting transfers between devices: none -> 40.8 us  [the longest x7 36.1 us: gather_around(): later.append(lax.ppermute(later[-1], axis, down))]
    ppermute x0 -> x15, waiting for transfers between devices: none -> 14.4 us  [the longest x8 14.4 us: gather_around(): earlier.append(lax.ppermute(earlier[-1], axis, up))]
    all_to_all x1, starting transfers between devices: 7.3 us -> 2.54 us  [body(): lax.all_to_all(geo_send, ('tx', 'ty'), split_axis=0, concat_axis=0, tiled...]
    all_to_all x1, waiting for transfers between devices: 2.56 us -> 7.3 us  [body(): lax.all_to_all(windows, ('tx', 'ty'), split_axis=0, concat_axis=0, tiled=...]
    concatenate x0 -> x1, local copies, waits for them, and re-layouts: none -> 1.39 us  [gather_around(): jnp.roll(line, (lax.axis_index(axis) - ways // 2) * x.shape[dim], axis=dim)]
  transfers between devices with their start and end apart: 2 -> 17, of which waited for: 1 -> 7; matrix products, arithmetic and copies ran while one was open for 40% -> 6% of each run, Pallas kernels for 0% -> 0%
where the time goes in v1:
time: 115 us; the launch traced here: 114 us
  starting transfers between devices  45.9 us (40%)
  local copies, waits for them, and re-layouts  36.4 us (32%)
  waiting for transfers between devices  21.7 us (19%)
  other arithmetic  8.94 us (8%)
    ppermute x7, starting transfers between devices, gather_around(): later.append(lax.ppermute(later[-1], axis, down))  36.1 us
    gather x48, local copies, waits for them, and re-layouts  32.2 us
    ppermute x8, waiting for transfers between devices, gather_around(): earlier.append(lax.ppermute(earlier[-1], axis, up))  14.4 us
    all_to_all x1, waiting for transfers between devices, body(): lax.all_to_all(windows, ('tx', 'ty'), split_axis=0, concat_axis=0, tiled=...  7.3 us
    ppermute x8, starting transfers between devices, gather_around(): earlier.append(lax.ppermute(earlier[-1], axis, up))  4.7 us
    another operation x3, other arithmetic  4.1 us
    all_to_all x1, starting transfers between devices, body(): lax.all_to_all(windows, ('tx', 'ty'), split_axis=0, concat_axis=0, tiled=...  2.57 us
    all_to_all x1, starting transfers between devices, body(): lax.all_to_all(geo_send, ('tx', 'ty'), split_axis=0, concat_axis=0, tiled...  2.54 us
  transfers between devices with their start and end apart: 17, of which 7 were waited for; matrix products, arithmetic and copies ran while one was open for 6% of the time, Pallas kernels for 0%

profile of v1, /device:TPU:0, one launch (start us, length us, event | category | flops | bytes accessed | tf_op | source)
XLA Modules:
  0.0 113.6 jit_solution(15495692862578484601)
XLA Ops:
  0.0 2.9 %collective-permute-start = (s32[32,1]{0,1:T(1,128)}, s32[32,1]{0,1:T(1,128)S(1)}, u32[]{:S(2)}, u32[]{:S(2)}) collective-permute-start(s32[32,1]{0,1:T(1,128)} %param.8), channel_id=1, source_target_pairs={{0,2},{2,4},{4,6},{6,8},{8,10},{10,12},{12,14},{14,16},{16,18},{18... | collective-permute-start | bytes 392 | tf_op jit(solution)/shard_map/ppermute | solution.py:16
  2.9 4.0 %collective-permute-start.8 = (s32[32,1]{0,1:T(1,128)}, s32[32,1]{0,1:T(1,128)S(1)}, u32[]{:S(2)}, u32[]{:S(2)}) collective-permute-start(s32[32,1]{0,1:T(1,128)} %param.8), channel_id=1, source_target_pairs={{0,30},{2,0},{4,2},{6,4},{8,6},{10,8},{12,10},{14,12},{16,14},{18,... | collective-permute-start | bytes 392 | tf_op jit(solution)/shard_map/ppermute | solution.py:18
  6.9 1.3 %broadcast_in_dim.21 = bf16[32,1,5]{2,1,0:T(2,128)(2,1)} broadcast(bf16[5]{0:T(256)(128)(2,1)} %bitcast.68), dimensions={2} | broadcast | bytes 330 | tf_op jit(solution)/shard_map/broadcast_in_dim | solution.py:91
  8.2 2.5 %all-to-all-start = ((bf16[32,1,5]{2,1,0:T(2,128)(2,1)}), bf16[32,1,5]{2,1,0:T(2,128)(2,1)S(1)}, u32[]{:S(2)}, u32[]{:S(2)}) async-start(bf16[32,1,5]{2,1,0:T(2,128)(2,1)} %broadcast_in_dim.21), calls=%async_computation | async-start | bytes 32768 | tf_op jit(solution)/shard_map/all_to_all | solution.py:94
  10.8 0.7 fusion.51
  11.8 1.7 %collective-permute-start.1 = (s32[32,1]{0,1:T(1,128)S(1)}, s32[32,1]{0,1:T(1,128)S(1)}, u32[]{:S(2)}, u32[]{:S(2)}) collective-permute-start(s32[32,1]{0,1:T(1,128)S(1)} %collective-permute-done), channel_id=1, source_target_pairs={{0,2},{2,4},{4,6},{6,8},{8,10},{10,12},{12,14},{14,16},{16,18},{18... | collective-permute-start | bytes 392 | tf_op jit(solution)/shard_map/ppermute | solution.py:16
  13.5 4.0 %collective-permute-start.9 = (s32[32,1]{0,1:T(1,128)S(1)}, s32[32,1]{0,1:T(1,128)S(1)}, u32[]{:S(2)}, u32[]{:S(2)}) collective-permute-start(s32[32,1]{0,1:T(1,128)S(1)} %collective-permute-done.8), channel_id=1, source_target_pairs={{0,30},{2,0},{4,2},{6,4},{8,6},{10,8},{12,10},{14,12},{16,14},{18,... | collective-permute-start | bytes 392 | tf_op jit(solution)/shard_map/ppermute | solution.py:18
  17.5 1.5 %collective-permute-done.1 = s32[32,1]{0,1:T(1,128)S(1)} collective-permute-done((s32[32,1]{0,1:T(1,128)S(1)}, s32[32,1]{0,1:T(1,128)S(1)}, u32[]{:S(2)}, u32[]{:S(2)}) %collective-permute-start.1) | collective-permute-done | bytes 160 | tf_op jit(solution)/shard_map/ppermute | solution.py:16
  19.0 5.6 %collective-permute-start.10 = (s32[32,1]{0,1:T(1,128)S(1)}, s32[32,1]{0,1:T(1,128)S(1)}, u32[]{:S(2)}, u32[]{:S(2)}) collective-permute-start(s32[32,1]{0,1:T(1,128)S(1)} %collective-permute-done.9), channel_id=1, source_target_pairs={{0,30},{2,0},{4,2},{6,4},{8,6},{10,8},{12,10},{14,12},{16,14},{18,... | collective-permute-start | bytes 392 | tf_op jit(solution)/shard_map/ppermute | solution.py:18
  24.6 1.5 %collective-permute-done.2 = s32[32,1]{0,1:T(1,128)S(1)} collective-permute-done((s32[32,1]{0,1:T(1,128)S(1)}, s32[32,1]{0,1:T(1,128)S(1)}, u32[]{:S(2)}, u32[]{:S(2)}) %collective-permute-start.2) | collective-permute-done | bytes 160 | tf_op jit(solution)/shard_map/ppermute | solution.py:16
  26.1 5.6 %collective-permute-start.11 = (s32[32,1]{0,1:T(1,128)S(1)}, s32[32,1]{0,1:T(1,128)S(1)}, u32[]{:S(2)}, u32[]{:S(2)}) collective-permute-start(s32[32,1]{0,1:T(1,128)S(1)} %collective-permute-done.10), channel_id=1, source_target_pairs={{0,30},{2,0},{4,2},{6,4},{8,6},{10,8},{12,10},{14,12},{16,14},{18,... | collective-permute-start | bytes 392 | tf_op jit(solution)/shard_map/ppermute | solution.py:18
  31.7 1.5 %collective-permute-done.3 = s32[32,1]{0,1:T(1,128)S(1)} collective-permute-done((s32[32,1]{0,1:T(1,128)S(1)}, s32[32,1]{0,1:T(1,128)S(1)}, u32[]{:S(2)}, u32[]{:S(2)}) %collective-permute-start.3) | collective-permute-done | bytes 160 | tf_op jit(solution)/shard_map/ppermute | solution.py:16
  33.2 5.6 %collective-permute-start.12 = (s32[32,1]{0,1:T(1,128)S(1)}, s32[32,1]{0,1:T(1,128)S(1)}, u32[]{:S(2)}, u32[]{:S(2)}) collective-permute-start(s32[32,1]{0,1:T(1,128)S(1)} %collective-permute-done.11), channel_id=1, source_target_pairs={{0,30},{2,0},{4,2},{6,4},{8,6},{10,8},{12,10},{14,12},{16,14},{18,... | collective-permute-start | bytes 392 | tf_op jit(solution)/shard_map/ppermute | solution.py:18
  39.0 0.5 multiply_cosine_fusion
  39.5 3.8 %multiply_convert_fusion.1 = (bf16[32,8,512]{2,0,1:T(8,128)(2,1)S(1)}, bf16[32,8,512]{2,0,1:T(8,128)(2,1)S(1)}) fusion(f32[32,512]{1,0:T(8,128)S(1)} %get-tuple-element.35, f32[32,512]{1,0:T(8,128)S(1)} %get-tuple-element.37, f32[8]{0:T(128)S(1)} %convert_add_fusion, f32[32,512]{1,0:T(8,128)S(1)} %get-tuple-element.36), kind=kLoop, calls=%fused_computation.11 | loop fusion | flops 1441792 | bytes 720928 | tf_op jit(solution)/shard_map/convert.7
  43.4 5.6 %collective-permute-start.13 = (s32[32,1]{0,1:T(1,128)S(1)}, s32[32,1]{0,1:T(1,128)S(1)}, u32[]{:S(2)}, u32[]{:S(2)}) collective-permute-start(s32[32,1]{0,1:T(1,128)S(1)} %collective-permute-done.12), channel_id=1, source_target_pairs={{0,30},{2,0},{4,2},{6,4},{8,6},{10,8},{12,10},{14,12},{16,14},{18,... | collective-permute-start | bytes 392 | tf_op jit(solution)/shard_map/ppermute | solution.py:18
  49.0 1.5 %collective-permute-done.5 = s32[32,1]{0,1:T(1,128)S(1)} collective-permute-done((s32[32,1]{0,1:T(1,128)S(1)}, s32[32,1]{0,1:T(1,128)S(1)}, u32[]{:S(2)}, u32[]{:S(2)}) %collective-permute-start.5) | collective-permute-done | bytes 160 | tf_op jit(solution)/shard_map/ppermute | solution.py:16
  50.5 5.6 %collective-permute-start.14 = (s32[32,1]{0,1:T(1,128)S(1)}, s32[32,1]{0,1:T(1,128)S(1)}, u32[]{:S(2)}, u32[]{:S(2)}) collective-permute-start(s32[32,1]{0,1:T(1,128)S(1)} %collective-permute-done.13), channel_id=1, source_target_pairs={{0,30},{2,0},{4,2},{6,4},{8,6},{10,8},{12,10},{14,12},{16,14},{18,... | collective-permute-start | bytes 392 | tf_op jit(solution)/shard_map/ppermute | solution.py:18
  56.1 1.5 %collective-permute-done.6 = s32[32,1]{0,1:T(1,128)S(1)} collective-permute-done((s32[32,1]{0,1:T(1,128)S(1)}, s32[32,1]{0,1:T(1,128)S(1)}, u32[]{:S(2)}, u32[]{:S(2)}) %collective-permute-start.6) | collective-permute-done | bytes 160 | tf_op jit(solution)/shard_map/ppermute | solution.py:16
  58.0 6.8 %collective-permute-done.7 = s32[32,1]{0,1:T(1,128)S(1)} collective-permute-done((s32[32,1]{0,1:T(1,128)S(1)}, s32[32,1]{0,1:T(1,128)S(1)}, u32[]{:S(2)}, u32[]{:S(2)}) %collective-permute-start.7) | collective-permute-done | bytes 160 | tf_op jit(solution)/shard_map/ppermute | solution.py:16
  64.8 1.4 %concatenate.29 = s32[32,32]{0,1:T(8,128)S(1)} concatenate(s32[32,1]{0,1:T(1,128)S(1)} %collective-permute-done.7, s32[32,1]{0,1:T(1,128)S(1)} %collective-permute-done.6, s32[32,1]{0,1:T(1,128)S(1)} %collective-permute-done.5, s32[32,1]{0,1:T(1,128)S(1)} %collective-permute-done.4, s32[32,1]{0,1:T(1,128)S(1)} %collective-permute-done.3, s32[32,1]{0,1:T(1,128)S(1)} %collective-permute-done.2, ...), dimensions={1} | concatenate | bytes 8192 | tf_op jit(solution)/shard_map/jit(_roll_dynamic)/concatenate | solution.py:20
  66.4 32.2 %while.1 = (s32[]{:T(128)}, bf16[1,2,16384]{2,1,0:T(2,128)(2,1)}, s32[16,3]{0,1:T(4,128)S(1)}, bf16[16,2,1032]{2,1,0:T(2,128)(2,1)S(1)}, s32[]{:T(128)}) while((s32[]{:T(128)}, bf16[1,2,16384]{2,1,0:T(2,128)(2,1)}, s32[16,3]{0,1:T(4,128)S(1)}, bf16[16,2,1032]{2,1,0:T(2,128)(2,1)S(1)}, s32[]{:T(128)}) %tuple.32), condition=%wide.while_cond, body=%wide.while_body.sunk | while | flops 2 | bytes 8849 | solution.py:79
  67.0 1.4 %dynamic-slice_dynamic-update-slice_fusion.2 = bf16[16,2,1032]{2,1,0:T(2,128)(2,1)S(1)} fusion(bf16[16,2,1032]{2,1,0:T(2,128)(2,1)S(1)} %get-tuple-element.76, s32[]{:T(128)S(6)} %copy.78, bf16[1,2,16384]{2,1,0:T(2,128)(2,1)} %get-tuple-element.79, s32[]{:T(128)} %bitcast.62), kind=kLoop, calls=%fused_computation.clone.1 | loop fusion | bytes 8744 | tf_op jit(solution)/shard_map/vmap(vmap())/gather
  68.5 0.5 slice.359
  69.0 1.4 %dynamic-slice_dynamic-update-slice_fusion.2 = bf16[16,2,1032]{2,1,0:T(2,128)(2,1)S(1)} fusion(bf16[16,2,1032]{2,1,0:T(2,128)(2,1)S(1)} %get-tuple-element.76, s32[]{:T(128)S(6)} %copy.78, bf16[1,2,16384]{2,1,0:T(2,128)(2,1)} %get-tuple-element.79, s32[]{:T(128)} %bitcast.62), kind=kLoop, calls=%fused_computation.clone.1 | loop fusion | bytes 8744 | tf_op jit(solution)/shard_map/vmap(vmap())/gather
  70.5 0.5 slice.359
  71.0 1.4 %dynamic-slice_dynamic-update-slice_fusion.2 = bf16[16,2,1032]{2,1,0:T(2,128)(2,1)S(1)} fusion(bf16[16,2,1032]{2,1,0:T(2,128)(2,1)S(1)} %get-tuple-element.76, s32[]{:T(128)S(6)} %copy.78, bf16[1,2,16384]{2,1,0:T(2,128)(2,1)} %get-tuple-element.79, s32[]{:T(128)} %bitcast.62), kind=kLoop, calls=%fused_computation.clone.1 | loop fusion | bytes 8744 | tf_op jit(solution)/shard_map/vmap(vmap())/gather
  72.5 0.5 slice.359
  73.0 1.4 %dynamic-slice_dynamic-update-slice_fusion.2 = bf16[16,2,1032]{2,1,0:T(2,128)(2,1)S(1)} fusion(bf16[16,2,1032]{2,1,0:T(2,128)(2,1)S(1)} %get-tuple-element.76, s32[]{:T(128)S(6)} %copy.78, bf16[1,2,16384]{2,1,0:T(2,128)(2,1)} %get-tuple-element.79, s32[]{:T(128)} %bitcast.62), kind=kLoop, calls=%fused_computation.clone.1 | loop fusion | bytes 8744 | tf_op jit(solution)/shard_map/vmap(vmap())/gather
  74.5 0.5 slice.359
  75.0 1.4 %dynamic-slice_dynamic-update-slice_fusion.2 = bf16[16,2,1032]{2,1,0:T(2,128)(2,1)S(1)} fusion(bf16[16,2,1032]{2,1,0:T(2,128)(2,1)S(1)} %get-tuple-element.76, s32[]{:T(128)S(6)} %copy.78, bf16[1,2,16384]{2,1,0:T(2,128)(2,1)} %get-tuple-element.79, s32[]{:T(128)} %bitcast.62), kind=kLoop, calls=%fused_computation.clone.1 | loop fusion | bytes 8744 | tf_op jit(solution)/shard_map/vmap(vmap())/gather
  76.5 0.5 slice.359
  77.0 1.4 %dynamic-slice_dynamic-update-slice_fusion.2 = bf16[16,2,1032]{2,1,0:T(2,128)(2,1)S(1)} fusion(bf16[16,2,1032]{2,1,0:T(2,128)(2,1)S(1)} %get-tuple-element.76, s32[]{:T(128)S(6)} %copy.78, bf16[1,2,16384]{2,1,0:T(2,128)(2,1)} %get-tuple-element.79, s32[]{:T(128)} %bitcast.62), kind=kLoop, calls=%fused_computation.clone.1 | loop fusion | bytes 8744 | tf_op jit(solution)/shard_map/vmap(vmap())/gather
  79.0 1.4 %dynamic-slice_dynamic-update-slice_fusion.2 = bf16[16,2,1032]{2,1,0:T(2,128)(2,1)S(1)} fusion(bf16[16,2,1032]{2,1,0:T(2,128)(2,1)S(1)} %get-tuple-element.76, s32[]{:T(128)S(6)} %copy.78, bf16[1,2,16384]{2,1,0:T(2,128)(2,1)} %get-tuple-element.79, s32[]{:T(128)} %bitcast.62), kind=kLoop, calls=%fused_computation.clone.1 | loop fusion | bytes 8744 | tf_op jit(solution)/shard_map/vmap(vmap())/gather
  81.1 1.4 %dynamic-slice_dynamic-update-slice_fusion.2 = bf16[16,2,1032]{2,1,0:T(2,128)(2,1)S(1)} fusion(bf16[16,2,1032]{2,1,0:T(2,128)(2,1)S(1)} %get-tuple-element.76, s32[]{:T(128)S(6)} %copy.78, bf16[1,2,16384]{2,1,0:T(2,128)(2,1)} %get-tuple-element.79, s32[]{:T(128)} %bitcast.62), kind=kLoop, calls=%fused_computation.clone.1 | loop fusion | bytes 8744 | tf_op jit(solution)/shard_map/vmap(vmap())/gather
  83.1 1.4 %dynamic-slice_dynamic-update-slice_fusion.2 = bf16[16,2,1032]{2,1,0:T(2,128)(2,1)S(1)} fusion(bf16[16,2,1032]{2,1,0:T(2,128)(2,1)S(1)} %get-tuple-element.76, s32[]{:T(128)S(6)} %copy.78, bf16[1,2,16384]{2,1,0:T(2,128)(2,1)} %get-tuple-element.79, s32[]{:T(128)} %bitcast.62), kind=kLoop, calls=%fused_computation.clone.1 | loop fusion | bytes 8744 | tf_op jit(solution)/shard_map/vmap(vmap())/gather
  85.1 1.4 %dynamic-slice_dynamic-update-slice_fusion.2 = bf16[16,2,1032]{2,1,0:T(2,128)(2,1)S(1)} fusion(bf16[16,2,1032]{2,1,0:T(2,128)(2,1)S(1)} %get-tuple-element.76, s32[]{:T(128)S(6)} %copy.78, bf16[1,2,16384]{2,1,0:T(2,128)(2,1)} %get-tuple-element.79, s32[]{:T(128)} %bitcast.62), kind=kLoop, calls=%fused_computation.clone.1 | loop fusion | bytes 8744 | tf_op jit(solution)/shard_map/vmap(vmap())/gather
  87.1 1.4 %dynamic-slice_dynamic-update-slice_fusion.2 = bf16[16,2,1032]{2,1,0:T(2,128)(2,1)S(1)} fusion(bf16[16,2,1032]{2,1,0:T(2,128)(2,1)S(1)} %get-tuple-element.76, s32[]{:T(128)S(6)} %copy.78, bf16[1,2,16384]{2,1,0:T(2,128)(2,1)} %get-tuple-element.79, s32[]{:T(128)} %bitcast.62), kind=kLoop, calls=%fused_computation.clone.1 | loop fusion | bytes 8744 | tf_op jit(solution)/shard_map/vmap(vmap())/gather
  89.1 1.4 %dynamic-slice_dynamic-update-slice_fusion.2 = bf16[16,2,1032]{2,1,0:T(2,128)(2,1)S(1)} fusion(bf16[16,2,1032]{2,1,0:T(2,128)(2,1)S(1)} %get-tuple-element.76, s32[]{:T(128)S(6)} %copy.78, bf16[1,2,16384]{2,1,0:T(2,128)(2,1)} %get-tuple-element.79, s32[]{:T(128)} %bitcast.62), kind=kLoop, calls=%fused_computation.clone.1 | loop fusion | bytes 8744 | tf_op jit(solution)/shard_map/vmap(vmap())/gather
  91.1 1.4 %dynamic-slice_dynamic-update-slice_fusion.2 = bf16[16,2,1032]{2,1,0:T(2,128)(2,1)S(1)} fusion(bf16[16,2,1032]{2,1,0:T(2,128)(2,1)S(1)} %get-tuple-element.76, s32[]{:T(128)S(6)} %copy.78, bf16[1,2,16384]{2,1,0:T(2,128)(2,1)} %get-tuple-element.79, s32[]{:T(128)} %bitcast.62), kind=kLoop, calls=%fused_computation.clone.1 | loop fusion | bytes 8744 | tf_op jit(solution)/shard_map/vmap(vmap())/gather
  93.1 1.4 %dynamic-slice_dynamic-update-slice_fusion.2 = bf16[16,2,1032]{2,1,0:T(2,128)(2,1)S(1)} fusion(bf16[16,2,1032]{2,1,0:T(2,128)(2,1)S(1)} %get-tuple-element.76, s32[]{:T(128)S(6)} %copy.78, bf16[1,2,16384]{2,1,0:T(2,128)(2,1)} %get-tuple-element.79, s32[]{:T(128)} %bitcast.62), kind=kLoop, calls=%fused_computation.clone.1 | loop fusion | bytes 8744 | tf_op jit(solution)/shard_map/vmap(vmap())/gather
  95.1 1.4 %dynamic-slice_dynamic-update-slice_fusion.2 = bf16[16,2,1032]{2,1,0:T(2,128)(2,1)S(1)} fusion(bf16[16,2,1032]{2,1,0:T(2,128)(2,1)S(1)} %get-tuple-element.76, s32[]{:T(128)S(6)} %copy.78, bf16[1,2,16384]{2,1,0:T(2,128)(2,1)} %get-tuple-element.79, s32[]{:T(128)} %bitcast.62), kind=kLoop, calls=%fused_computation.clone.1 | loop fusion | bytes 8744 | tf_op jit(solution)/shard_map/vmap(vmap())/gather
  97.2 1.4 %dynamic-slice_dynamic-update-slice_fusion.2 = bf16[16,2,1032]{2,1,0:T(2,128)(2,1)S(1)} fusion(bf16[16,2,1032]{2,1,0:T(2,128)(2,1)S(1)} %get-tuple-element.76, s32[]{:T(128)S(6)} %copy.78, bf16[1,2,16384]{2,1,0:T(2,128)(2,1)} %get-tuple-element.79, s32[]{:T(128)} %bitcast.62), kind=kLoop, calls=%fused_computation.clone.1 | loop fusion | bytes 8744 | tf_op jit(solution)/shard_map/vmap(vmap())/gather
  98.8 0.8 fusion.11
  99.6 2.6 %all-to-all-start.1 = ((bf16[32,1,2,520]{3,2,1,0:T(2,128)(2,1)}), bf16[32,1,2,520]{3,2,1,0:T(2,128)(2,1)S(1)}, u32[]{:S(2)}, u32[]{:S(2)}) async-start(bf16[32,1,2,520]{3,2,1,0:T(2,128)(2,1)} %fusion.11), calls=%async_computation.1 | async-start | bytes 163840 | tf_op jit(solution)/shard_map/all_to_all | solution.py:93
  102.5 7.3 %all-to-all-done.1 = bf16[32,1,2,520]{3,2,1,0:T(2,128)(2,1)S(1)} async-done(((bf16[32,1,2,520]{3,2,1,0:T(2,128)(2,1)}), bf16[32,1,2,520]{3,2,1,0:T(2,128)(2,1)S(1)}, u32[]{:S(2)}, u32[]{:S(2)}) %all-to-all-start.1) | async-done | bytes 66592 | tf_op jit(solution)/shard_map/all_to_all | solution.py:93
  110.9 0.9 copy-done
  111.8 1.8 %add.219 = f32[2,512,512]{2,1,0:T(8,128)} add(f32[2,512,512]{2,1,0:T(8,128)S(1)} %copy-done, f32[2,512,512]{2,1,0:T(8,128)S(1)} %bitcast.63) | non-fusion elementwise | flops 524288 | bytes 6291456 | tf_op jit(solution)/shard_map/add | solution.py:112
  (65 shorter events, 9.3 us)
Async XLA Ops:
  0.0 11.8 %collective-permute-start = (s32[32,1]{0,1:T(1,128)}, s32[32,1]{0,1:T(1,128)S(1)}, u32[]{:S(2)}, u32[]{:S(2)}) collective-permute-start(s32[32,1]{0,1:T(1,128)} %param.8), channel_id=1, source_target_pairs={{0,2},{2,4},{4,6},{6,8},{8,10},{10,12},{12,14},{14,16},{16,18},{18... | collective-permute-start | bytes 392 | tf_op jit(solution)/shard_map/ppermute | solution.py:16
  2.9 10.5 %collective-permute-start.8 = (s32[32,1]{0,1:T(1,128)}, s32[32,1]{0,1:T(1,128)S(1)}, u32[]{:S(2)}, u32[]{:S(2)}) collective-permute-start(s32[32,1]{0,1:T(1,128)} %param.8), channel_id=1, source_target_pairs={{0,30},{2,0},{4,2},{6,4},{8,6},{10,8},{12,10},{14,12},{16,14},{18,... | collective-permute-start | bytes 392 | tf_op jit(solution)/shard_map/ppermute | solution.py:18
  8.2 30.7 %all-to-all-start = ((bf16[32,1,5]{2,1,0:T(2,128)(2,1)}), bf16[32,1,5]{2,1,0:T(2,128)(2,1)S(1)}, u32[]{:S(2)}, u32[]{:S(2)}) async-start(bf16[32,1,5]{2,1,0:T(2,128)(2,1)} %broadcast_in_dim.21), calls=%async_computation | async-start | bytes 32768 | tf_op jit(solution)/shard_map/all_to_all | solution.py:94
  11.8 7.2 %collective-permute-start.1 = (s32[32,1]{0,1:T(1,128)S(1)}, s32[32,1]{0,1:T(1,128)S(1)}, u32[]{:S(2)}, u32[]{:S(2)}) collective-permute-start(s32[32,1]{0,1:T(1,128)S(1)} %collective-permute-done), channel_id=1, source_target_pairs={{0,2},{2,4},{4,6},{6,8},{8,10},{10,12},{12,14},{14,16},{16,18},{18... | collective-permute-start | bytes 392 | tf_op jit(solution)/shard_map/ppermute | solution.py:16
  13.5 5.5 %collective-permute-start.9 = (s32[32,1]{0,1:T(1,128)S(1)}, s32[32,1]{0,1:T(1,128)S(1)}, u32[]{:S(2)}, u32[]{:S(2)}) collective-permute-start(s32[32,1]{0,1:T(1,128)S(1)} %collective-permute-done.8), channel_id=1, source_target_pairs={{0,30},{2,0},{4,2},{6,4},{8,6},{10,8},{12,10},{14,12},{16,14},{18,... | collective-permute-start | bytes 392 | tf_op jit(solution)/shard_map/ppermute | solution.py:18
  19.0 7.1 %collective-permute-start.2 = (s32[32,1]{0,1:T(1,128)S(1)}, s32[32,1]{0,1:T(1,128)S(1)}, u32[]{:S(2)}, u32[]{:S(2)}) collective-permute-start(s32[32,1]{0,1:T(1,128)S(1)} %collective-permute-done.1), channel_id=1, source_target_pairs={{0,2},{2,4},{4,6},{6,8},{8,10},{10,12},{12,14},{14,16},{16,18},{18... | collective-permute-start | bytes 392 | tf_op jit(solution)/shard_map/ppermute | solution.py:16
  19.0 7.1 %collective-permute-start.10 = (s32[32,1]{0,1:T(1,128)S(1)}, s32[32,1]{0,1:T(1,128)S(1)}, u32[]{:S(2)}, u32[]{:S(2)}) collective-permute-start(s32[32,1]{0,1:T(1,128)S(1)} %collective-permute-done.9), channel_id=1, source_target_pairs={{0,30},{2,0},{4,2},{6,4},{8,6},{10,8},{12,10},{14,12},{16,14},{18,... | collective-permute-start | bytes 392 | tf_op jit(solution)/shard_map/ppermute | solution.py:18
  26.1 7.1 %collective-permute-start.3 = (s32[32,1]{0,1:T(1,128)S(1)}, s32[32,1]{0,1:T(1,128)S(1)}, u32[]{:S(2)}, u32[]{:S(2)}) collective-permute-start(s32[32,1]{0,1:T(1,128)S(1)} %collective-permute-done.2), channel_id=1, source_target_pairs={{0,2},{2,4},{4,6},{6,8},{8,10},{10,12},{12,14},{14,16},{16,18},{18... | collective-permute-start | bytes 392 | tf_op jit(solution)/shard_map/ppermute | solution.py:16
  26.1 7.1 %collective-permute-start.11 = (s32[32,1]{0,1:T(1,128)S(1)}, s32[32,1]{0,1:T(1,128)S(1)}, u32[]{:S(2)}, u32[]{:S(2)}) collective-permute-start(s32[32,1]{0,1:T(1,128)S(1)} %collective-permute-done.10), channel_id=1, source_target_pairs={{0,30},{2,0},{4,2},{6,4},{8,6},{10,8},{12,10},{14,12},{16,14},{18,... | collective-permute-start | bytes 392 | tf_op jit(solution)/shard_map/ppermute | solution.py:18
  33.2 10.1 %collective-permute-start.4 = (s32[32,1]{0,1:T(1,128)S(1)}, s32[32,1]{0,1:T(1,128)S(1)}, u32[]{:S(2)}, u32[]{:S(2)}) collective-permute-start(s32[32,1]{0,1:T(1,128)S(1)} %collective-permute-done.3), channel_id=1, source_target_pairs={{0,2},{2,4},{4,6},{6,8},{8,10},{10,12},{12,14},{14,16},{16,18},{18... | collective-permute-start | bytes 392 | tf_op jit(solution)/shard_map/ppermute | solution.py:16
  33.2 10.1 %collective-permute-start.12 = (s32[32,1]{0,1:T(1,128)S(1)}, s32[32,1]{0,1:T(1,128)S(1)}, u32[]{:S(2)}, u32[]{:S(2)}) collective-permute-start(s32[32,1]{0,1:T(1,128)S(1)} %collective-permute-done.11), channel_id=1, source_target_pairs={{0,30},{2,0},{4,2},{6,4},{8,6},{10,8},{12,10},{14,12},{16,14},{18,... | collective-permute-start | bytes 392 | tf_op jit(solution)/shard_map/ppermute | solution.py:18
  43.3 7.2 %collective-permute-start.5 = (s32[32,1]{0,1:T(1,128)S(1)}, s32[32,1]{0,1:T(1,128)S(1)}, u32[]{:S(2)}, u32[]{:S(2)}) collective-permute-start(s32[32,1]{0,1:T(1,128)S(1)} %collective-permute-done.4), channel_id=1, source_target_pairs={{0,2},{2,4},{4,6},{6,8},{8,10},{10,12},{12,14},{14,16},{16,18},{18... | collective-permute-start | bytes 392 | tf_op jit(solution)/shard_map/ppermute | solution.py:16
  43.4 7.1 %collective-permute-start.13 = (s32[32,1]{0,1:T(1,128)S(1)}, s32[32,1]{0,1:T(1,128)S(1)}, u32[]{:S(2)}, u32[]{:S(2)}) collective-permute-start(s32[32,1]{0,1:T(1,128)S(1)} %collective-permute-done.12), channel_id=1, source_target_pairs={{0,30},{2,0},{4,2},{6,4},{8,6},{10,8},{12,10},{14,12},{16,14},{18,... | collective-permute-start | bytes 392 | tf_op jit(solution)/shard_map/ppermute | solution.py:18
  50.5 7.1 %collective-permute-start.6 = (s32[32,1]{0,1:T(1,128)S(1)}, s32[32,1]{0,1:T(1,128)S(1)}, u32[]{:S(2)}, u32[]{:S(2)}) collective-permute-start(s32[32,1]{0,1:T(1,128)S(1)} %collective-permute-done.5), channel_id=1, source_target_pairs={{0,2},{2,4},{4,6},{6,8},{8,10},{10,12},{12,14},{14,16},{16,18},{18... | collective-permute-start | bytes 392 | tf_op jit(solution)/shard_map/ppermute | solution.py:16
  50.5 7.5 %collective-permute-start.14 = (s32[32,1]{0,1:T(1,128)S(1)}, s32[32,1]{0,1:T(1,128)S(1)}, u32[]{:S(2)}, u32[]{:S(2)}) collective-permute-start(s32[32,1]{0,1:T(1,128)S(1)} %collective-permute-done.13), channel_id=1, source_target_pairs={{0,30},{2,0},{4,2},{6,4},{8,6},{10,8},{12,10},{14,12},{16,14},{18,... | collective-permute-start | bytes 392 | tf_op jit(solution)/shard_map/ppermute | solution.py:18
  57.6 7.1 %collective-permute-start.7 = (s32[32,1]{0,1:T(1,128)S(1)}, s32[32,1]{0,1:T(1,128)S(1)}, u32[]{:S(2)}, u32[]{:S(2)}) collective-permute-start(s32[32,1]{0,1:T(1,128)S(1)} %collective-permute-done.6), channel_id=1, source_target_pairs={{0,2},{2,4},{4,6},{6,8},{8,10},{10,12},{12,14},{14,16},{16,18},{18... | collective-permute-start | bytes 392 | tf_op jit(solution)/shard_map/ppermute | solution.py:16
  99.6 10.2 %all-to-all-start.1 = ((bf16[32,1,2,520]{3,2,1,0:T(2,128)(2,1)}), bf16[32,1,2,520]{3,2,1,0:T(2,128)(2,1)S(1)}, u32[]{:S(2)}, u32[]{:S(2)}) async-start(bf16[32,1,2,520]{3,2,1,0:T(2,128)(2,1)} %fusion.11), calls=%async_computation.1 | async-start | bytes 163840 | tf_op jit(solution)/shard_map/all_to_all | solution.py:93
  110.2 1.6 %copy-start = (f32[2,512,512]{2,1,0:T(8,128)S(1)}, f32[2,512,512]{2,1,0:T(8,128)}, u32[]{:S(2)}) copy-start(f32[2,512,512]{2,1,0:T(8,128)} %param.9) | copy-start | bytes 6291460
